TPU v7x, 32 devices: a whole 2x2x4 slice. The times are simulated.
32 devices in a mesh: cell: 4 (over y, x), blk: 8 (over z, core).
Axes of the slice: x: 2, y: 2, z: 4, core: 2. Of those that a mesh axis runs over, the one named last changes fastest.
Arguments:
- codes: bfloat16 [16384, 128], P(('cell', 'blk')), may hold values from -60 to 60
- scales: float32 [16384], P(('cell', 'blk')), may hold values from 0.5 to 2
- coarse_ids: int32 [16384], P(('cell', 'blk')), may hold values from 0 to 3, as said below
- centroids: bfloat16 [32768, 128], P(('cell', 'blk')), may hold values from -6 to 6
Outputs:
- reconstruction: bfloat16 [16384, 128], P(('cell', 'blk'))
- residual: bfloat16 [16384, 128], P(('cell', 'blk'))
Inputs may be any that keep to these rules, and one draw needn't show every extreme that they name: `coarse_ids`: on every device, the number of its 512 rows that name partition g is the same for all devices; at most 256 rows of one device name one partition, and one partition is named by exactly 256 rows of every device.
All inputs are finite; a program needn't handle non-finite values.
Results may differ from a plain program's by a relative error of at most 0.006.
Values may be sent and summed in bfloat16 or wider, within the bound.
No kernel may reach another device: no remote copies, remote signals or barrier semaphores. Data moves between devices by JAX's collectives and lax.ppermute only.
A program may use at most 256 MiB of HBM per device.

v0:
```python
import math
import jax
import jax.numpy as jnp
from jax import lax
from jax.sharding import PartitionSpec as P


def local(codes, scales, coarse_ids, centroids):
    rows_dev = codes.shape[0]
    width = codes.shape[1]
    loops = lax.axis_size("cell")
    cap = 2 * rows_dev // loops
    beta = 1.0 / math.sqrt(width)
    dequant = (codes.astype(jnp.float32) * scales[:, None]).astype(jnp.bfloat16)
    onehot = (coarse_ids[:, None] == jnp.arange(loops, dtype=jnp.int32)[None, :]).astype(jnp.int32)
    ranks = jnp.sum(jnp.cumsum(onehot, axis=0) * onehot, axis=1) - 1
    slots = coarse_ids * cap + ranks
    outgoing = jnp.zeros((loops * cap, width), jnp.bfloat16).at[slots].set(dequant)
    arrived = lax.all_to_all(
        outgoing.reshape(loops, cap, width), "cell", split_axis=0, concat_axis=0, tiled=True
    )
    queries = arrived.reshape(loops * cap, width)

    def scores_of(piece):
        product = lax.dot_general(
            queries, piece, (((1,), (1,)), ((), ())), preferred_element_type=jnp.float32
        )
        return product * beta

    top = jnp.max(scores_of(lax.all_gather(centroids, "blk", axis=0, tiled=True)), axis=1)
    piece = lax.all_gather(centroids, "blk", axis=0, tiled=True)
    weights = jnp.exp(scores_of(piece) - top[:, None]).astype(jnp.bfloat16)
    total = jnp.sum(weights.astype(jnp.float32), axis=1)
    numer = jnp.dot(weights, piece, preferred_element_type=jnp.float32)
    total, numer = (total, numer)
    recon = (numer / total[:, None]).astype(jnp.bfloat16)
    remote_residual = (queries.astype(jnp.float32) - recon.astype(jnp.float32)).astype(jnp.bfloat16)
    stacked = jnp.stack([recon, remote_residual]).reshape(2, loops, cap, width)
    back = lax.all_to_all(stacked, "cell", split_axis=1, concat_axis=1, tiled=True).reshape(
        2, loops * cap, width
    )
    return (back[0][slots], back[1][slots])


def solution(mesh):
    in_specs = (
        P(("cell", "blk"), None),
        P(("cell", "blk")),
        P(("cell", "blk")),
        P(("cell", "blk"), None),
    )
    out_specs = (P(("cell", "blk"), None), P(("cell", "blk"), None))
    return jax.shard_map(local, mesh=mesh, in_specs=in_specs, out_specs=out_specs, check_vma=False)
```

profile of v0, /device:TPU:0, one launch (start us, length us, event | category | flops | bytes accessed | tf_op | source)
XLA Modules:
  0.0 99.3 jit_solution(16947095340633523881)
XLA Ops:
  7.2 0.0 all-gather.2.cloned.1.call-start
  7.2 0.7 all-gather.2.cloned.1.call-update
  7.9 0.7 fusion.6
  8.6 1.2 %reduce-window.6 = s32[4,4,128]{2,1,0:T(4,128)S(1)} reduce-window(s32[4,4,128]{2,1,0:T(4,128)S(1)} %fusion.6, s32[]{:T(128)} %constant.4.clone.1), window={size=1x1x128 pad=0_0x0_0x127_0}, to_apply=%region_0.0 | reduce-window | flops 260096 | bytes 16388 | tf_op jit(solution)/shard_map/reduce-window
  9.8 0.2 slice_reduce_fusion
  10.0 0.2 reduce-window.9
  10.2 0.1 add_bitcast_fusion
  10.3 0.7 fusion.5
  11.0 0.7 compare_select_fusion
  11.7 2.3 %scatter_custom_fusion = bf16[1024,128]{1,0:T(8,128)(2,1)S(1)} fusion(s32[512]{0:T(512)S(1)} %compare_select_fusion, bf16[512,128]{1,0:T(8,128)(2,1)} %param.4, f32[512]{0:T(512)} %param.5, bf16[]{:T(256)} %constant.8.clone.1), kind=kCustom, calls=%fused_computation.11 | custom fusion | flops 196608 | bytes 395266 | tf_op jit(solution)/shard_map/scatter | solution.py:18
  14.0 10.7 %all_to_all.10 = bf16[4,256,128]{2,1,0:T(8,128)(2,1)S(1)} all-to-all(bf16[4,256,128]{2,1,0:T(8,128)(2,1)S(1)} %bitcast.34), channel_id=1, replica_groups=mesh['cell'=4,'blk'=8] {'cell'}, dimensions={0} | all-to-all | bytes 524288 | tf_op jit(solution)/shard_map/all_to_all | solution.py:19
  24.7 16.8 %all-gather.2.cloned.1.call-done = bf16[8192,128]{1,0:T(8,128)(2,1)} async-done(((bf16[1024,128]{1,0:T(8,128)(2,1)}), bf16[8192,128]{1,0:T(8,128)(2,1)}) %all-gather.2.cloned.1.call-update) | async-done | bytes 2097168 | tf_op jit(solution)/shard_map/all_gather | solution.py:31
  41.5 14.6 %multiply_reduce_fusion = (f32[1024]{0:T(1024)S(1)}, f32[1024,8192]{1,0:T(8,128)}) fusion(bf16[1024,128]{1,0:T(8,128)(2,1)S(1)} %bitcast.33, bf16[8192,128]{1,0:T(8,128)(2,1)} %all-gather.2.cloned.1.call-done), kind=kOutput, calls=%fused_computation.5 | convolution fusion | flops 2164259840 | bytes 35917824 | tf_op jit(solution)/shard_map/dot_general | solution.py:25
  56.1 0.0 copy-start
  56.1 15.0 %convert_reduce_fusion = (f32[1024]{0:T(1024)S(1)}, bf16[1024,8192]{1,0:T(8,128)(2,1)S(1)}) fusion(f32[1024]{0:T(1024)S(1)} %get-tuple-element.6, f32[1024,8192]{1,0:T(8,128)} %get-tuple-element.7), kind=kLoop, calls=%fused_computation.3 | loop fusion | flops 41942016 | bytes 50339840 | tf_op jit(solution)/shard_map/reduce_sum | solution.py:33
  71.1 0.0 copy-done
  71.1 4.5 %subtract_convert_fusion = (bf16[1024,128]{1,0:T(8,128)(2,1)S(1)}, bf16[1024,128]{1,0:T(8,128)(2,1)S(1)}) fusion(bf16[4,256,128]{2,1,0:T(8,128)(2,1)S(1)} %all_to_all.10, f32[1024]{0:T(1024)S(1)} %get-tuple-element.2, bf16[1024,8192]{1,0:T(8,128)(2,1)S(1)} %get-tuple-element.3, bf16[8192,128]{1,0:T(8,128)(2,1)S(1)} %copy-done), kind=kOutput, calls=%fused_computation.9 | convolution fusion | flops 2148270080 | bytes 19664896 | tf_op jit(solution)/shard_map/dot_general | solution.py:34
  75.6 0.8 pad_maximum_fusion
  76.4 3.6 %all-to-all-start.1 = ((bf16[2,4,256,128]{3,2,0,1:T(8,128)(2,1)}), bf16[2,4,256,128]{3,2,0,1:T(8,128)(2,1)S(1)}, u32[]{:S(2)}, u32[]{:S(2)}) async-start(bf16[2,4,256,128]{3,2,0,1:T(8,128)(2,1)} %pad_maximum_fusion), calls=%async_computation.1 | async-start | bytes 1048576 | tf_op jit(solution)/shard_map/all_to_all | solution.py:39
  80.1 8.5 %all-to-all-done.1 = bf16[2,4,256,128]{3,2,0,1:T(8,128)(2,1)S(1)} async-done(((bf16[2,4,256,128]{3,2,0,1:T(8,128)(2,1)}), bf16[2,4,256,128]{3,2,0,1:T(8,128)(2,1)S(1)}, u32[]{:S(2)}, u32[]{:S(2)}) %all-to-all-start.1) | async-done | bytes 524320 | tf_op jit(solution)/shard_map/all_to_all | solution.py:39
  88.6 1.9 %gather_fusion.1 = bf16[512,128]{1,0:T(8,128)(2,1)} fusion(bf16[1024,128]{1,0:T(8,128)(2,1)S(1)} %bitcast.32, s32[1024]{0:T(1024)S(1)} %pad_clamp_fusion), kind=kCustom, calls=%fused_computation.1 | custom fusion | bytes 264192 | tf_op jit(solution)/shard_map/gather | solution.py:42
  90.5 1.9 %gather_fusion = bf16[512,128]{1,0:T(8,128)(2,1)} fusion(bf16[1024,128]{1,0:T(8,128)(2,1)S(1)} %bitcast.31, s32[1024]{0:T(1024)S(1)} %pad_clamp_fusion), kind=kCustom, calls=%fused_computation | custom fusion | bytes 264192 | tf_op jit(solution)/shard_map/gather | solution.py:42
  (2 shorter events, 0.0 us)
Async XLA Ops:
  7.2 34.3 %all-gather.2.cloned.1.call-start = ((), (), s32[]{:S(2)}) async-start(), calls=%async_computation.2 | async-start | bytes 2359296 | tf_op jit(solution)/shard_map/all_gather | solution.py:31
  56.1 15.0 %copy-start = (bf16[8192,128]{1,0:T(8,128)(2,1)S(1)}, bf16[8192,128]{1,0:T(8,128)(2,1)}, u32[]{:S(2)}) copy-start(bf16[8192,128]{1,0:T(8,128)(2,1)} %all-gather.2.cloned.1.call-done) | copy-start | bytes 6291460
  76.4 12.1 %all-to-all-start.1 = ((bf16[2,4,256,128]{3,2,0,1:T(8,128)(2,1)}), bf16[2,4,256,128]{3,2,0,1:T(8,128)(2,1)S(1)}, u32[]{:S(2)}, u32[]{:S(2)}) async-start(bf16[2,4,256,128]{3,2,0,1:T(8,128)(2,1)} %pad_maximum_fusion), calls=%async_computation.1 | async-start | bytes 1048576 | tf_op jit(solution)/shard_map/all_to_all | solution.py:39
Sparse Core Ops, SparseCore 0:
  9.6 31.8 all-gather.1
where the time goes:
time: 99.7 us; the launch traced here: 99.3 us
  waiting for transfers between devices  26 us (26%)
  other arithmetic  21.6 us (22%)
  matrix products  19.1 us (19%)
  between operations  14.1 us (14%)
  blocking collectives  10.7 us (11%)
  local copies, waits for them, and re-layouts  4.08 us (4%)
  starting transfers between devices  3.69 us (4%)
    all_gather x1, waiting for transfers between devices, local(): piece = lax.all_gather(centroids, 'blk', axis=0, tiled=True)  16.8 us
    reduce_sum x1, other arithmetic, local(): total = jnp.sum(weights.astype(jnp.float32), axis=1)  15 us
    dot_general x1, matrix products, scores_of(): lax.dot_general(queries, piece, (((1,), (1,)), ((), ())), preferred_eleme...  14.6 us
    all_to_all x1, blocking collectives, local(): lax.all_to_all(outgoing.reshape(loops, cap, width), 'cell', split_axis=0,...  10.7 us
    all_to_all x1, waiting for transfers between devices, local(): lax.all_to_all(stacked, 'cell', split_axis=1, concat_axis=1, tiled=True)  8.47 us
    dot_general x1, matrix products, local(): numer = jnp.dot(weights, piece, preferred_element_type=jnp.float32)  4.49 us
    gather x2, local copies, waits for them, and re-layouts, local(): return (back[0][slots], back[1][slots])  3.83 us
    all_to_all x1, starting transfers between devices, local(): lax.all_to_all(stacked, 'cell', split_axis=1, concat_axis=1, tiled=True)  3.65 us
  transfers between devices with their start and end apart: 2, of which 2 were waited for; matrix products, arithmetic and copies ran while one was open for 6% of the time, Pallas kernels for 0%

commit v1 on v0

--- a/solution.py
+++ b/solution.py
@@ -3,6 +3,37 @@
 import jax.numpy as jnp
 from jax import lax
 from jax.sharding import PartitionSpec as P
+
+
+def side_manage(my_tile, ndim_at, t0):
+    y1 = my_tile.shape
+    return jnp.moveaxis(
+        my_tile.reshape(*y1[:ndim_at], t0, y1[ndim_at] // t0, *y1[ndim_at + 1 :]), ndim_at, 0
+    )
+
+
+def pair_stocks_now(unit, array_dim):
+    unit = jnp.moveaxis(unit, 0, array_dim)
+    block_next = unit.shape
+    return unit.reshape(
+        *block_next[:array_dim],
+        block_next[array_dim] * block_next[array_dim + 1],
+        *block_next[array_dim + 2 :]
+    )
+
+
+def cut_the_matrix(x_in, which_axis, shard_in, own_rows):
+    moved, small = (lax.axis_size(which_axis), lax.axis_index(which_axis))
+    shaped = side_manage(x_in, shard_in, moved)
+    extra = shaped
+    for i in range(1, moved):
+        latest, value_now = ((small + i) % moved, (small - i) % moved)
+        built = lax.dynamic_index_in_dim(shaped, latest, 0)
+        block_last = lax.ppermute(
+            built, which_axis, list(map(lambda j0: (j0, (j0 + i) % moved), range(moved)))
+        )
+        extra = lax.dynamic_update_slice_in_dim(extra, block_last, value_now, axis=0)
+    return pair_stocks_now(extra, own_rows)
 
 
 def local(codes, scales, coarse_ids, centroids):
@@ -36,9 +67,7 @@
     recon = (numer / total[:, None]).astype(jnp.bfloat16)
     remote_residual = (queries.astype(jnp.float32) - recon.astype(jnp.float32)).astype(jnp.bfloat16)
     stacked = jnp.stack([recon, remote_residual]).reshape(2, loops, cap, width)
-    back = lax.all_to_all(stacked, "cell", split_axis=1, concat_axis=1, tiled=True).reshape(
-        2, loops * cap, width
-    )
+    back = cut_the_matrix(stacked, "cell", 1, 1).reshape(2, loops * cap, width)
     return (back[0][slots], back[1][slots])
 
 

time: 99.7 us -> 96.2 us (0.965)
  blocking collectives: 10.7 us -> 0 us
  starting transfers between devices: 3.69 us -> 9.73 us
  waiting for transfers between devices: 26 us -> 27.3 us
    all_to_all x1 -> x0, blocking collectives: 10.7 us -> none  [local(): lax.all_to_all(outgoing.reshape(loops, cap, width), 'cell', split_axis=0,...]
    ppermute x0 -> x3, waiting for transfers between devices: none -> 4.82 us  [cut_the_matrix(): lax.ppermute(built, which_axis, list(map(lambda j0: (j0, (j0 + i) % moved...]
    ppermute x0 -> x3, starting transfers between devices: none -> 4.51 us  [cut_the_matrix(): lax.ppermute(built, which_axis, list(map(lambda j0: (j0, (j0 + i) % moved...]
    all_to_all x1, waiting for transfers between devices: 8.47 us -> 5.37 us  [local(): lax.all_to_all(outgoing.reshape(loops, cap, width), 'cell', split_axis=0,...]
    all_to_all x1, starting transfers between devices: 3.65 us -> 5.19 us  [local(): lax.all_to_all(outgoing.reshape(loops, cap, width), 'cell', split_axis=0,...]
    another operation x3 -> x2, other arithmetic: 2.22 us -> 1.39 us
  transfers between devices with their start and end apart: 2 -> 5, of which waited for: 2 -> 4; matrix products, arithmetic and copies ran while one was open for 6% -> 7% of each run, Pallas kernels for 0% -> 0%
where the time goes in v1:
time: 96.2 us; the launch traced here: 95.8 us
  waiting for transfers between devices  27.3 us (28%)
  other arithmetic  21.5 us (22%)
  matrix products  19.1 us (20%)
  between operations  14.1 us (15%)
  starting transfers between devices  9.73 us (10%)
  local copies, waits for them, and re-layouts  4.14 us (4%)
    all_gather x1, waiting for transfers between devices, local(): piece = lax.all_gather(centroids, 'blk', axis=0, tiled=True)  16.4 us
    reduce_sum x1, other arithmetic, local(): total = jnp.sum(weights.astype(jnp.float32), axis=1)  15 us
    dot_general x1, matrix products, scores_of(): lax.dot_general(queries, piece, (((1,), (1,)), ((), ())), preferred_eleme...  14.6 us
    all_to_all x1, waiting for transfers between devices, local(): lax.all_to_all(outgoing.reshape(loops, cap, width), 'cell', split_axis=0,...  5.37 us
    all_to_all x1, starting transfers between devices, local(): lax.all_to_all(outgoing.reshape(loops, cap, width), 'cell', split_axis=0,...  5.19 us
    ppermute x3, waiting for transfers between devices, cut_the_matrix(): lax.ppermute(built, which_axis, list(map(lambda j0: (j0, (j0 + i) % moved...  4.82 us
    ppermute x3, starting transfers between devices, cut_the_matrix(): lax.ppermute(built, which_axis, list(map(lambda j0: (j0, (j0 + i) % moved...  4.51 us
    dot_general x1, matrix products, local(): numer = jnp.dot(weights, piece, preferred_element_type=jnp.float32)  4.49 us
  transfers between devices with their start and end apart: 5, of which 4 were waited for; matrix products, arithmetic and copies ran while one was open for 7% of the time, Pallas kernels for 0%

profile of v1, /device:TPU:0, one launch (start us, length us, event | category | flops | bytes accessed | tf_op | source)
XLA Modules:
  0.0 95.8 jit_solution(1031271490931670138)
XLA Ops:
  7.2 0.0 all-gather.2.cloned.1.call-start
  7.2 0.7 all-gather.2.cloned.1.call-update
  7.9 0.7 fusion.13
  8.6 1.2 %reduce-window.6 = s32[4,4,128]{2,1,0:T(4,128)S(1)} reduce-window(s32[4,4,128]{2,1,0:T(4,128)S(1)} %fusion.13, s32[]{:T(128)} %constant.64.clone.1), window={size=1x1x128 pad=0_0x0_0x127_0}, to_apply=%region_0.0 | reduce-window | flops 260096 | bytes 16388 | tf_op jit(solution)/shard_map/reduce-window
  9.8 0.2 slice_reduce_fusion
  10.0 0.2 reduce-window.9
  10.2 0.1 add_bitcast_fusion
  10.3 0.7 fusion.12
  11.0 0.7 compare_select_fusion
  11.7 2.9 %scatter_custom_fusion = bf16[1024,128]{1,0:T(8,128)(2,1)} fusion(s32[512]{0:T(512)S(1)} %compare_select_fusion, bf16[512,128]{1,0:T(8,128)(2,1)} %param.4, f32[512]{0:T(512)} %param.5, bf16[]{:T(256)} %constant.62.clone.1), kind=kCustom, calls=%fused_computation.18 | custom fusion | flops 196608 | bytes 395266 | tf_op jit(solution)/shard_map/scatter | solution.py:49
  14.5 5.2 %all-to-all-start = ((bf16[4,256,128]{2,1,0:T(8,128)(2,1)}), bf16[4,256,128]{2,1,0:T(8,128)(2,1)S(1)}, u32[]{:S(2)}, u32[]{:S(2)}) async-start(bf16[4,256,128]{2,1,0:T(8,128)(2,1)} %bitcast.2), calls=%async_computation | async-start | bytes 524288 | tf_op jit(solution)/shard_map/all_to_all | solution.py:50
  19.7 5.4 %all-to-all-done = bf16[4,256,128]{2,1,0:T(8,128)(2,1)S(1)} async-done(((bf16[4,256,128]{2,1,0:T(8,128)(2,1)}), bf16[4,256,128]{2,1,0:T(8,128)(2,1)S(1)}, u32[]{:S(2)}, u32[]{:S(2)}) %all-to-all-start) | async-done | bytes 262176 | tf_op jit(solution)/shard_map/all_to_all | solution.py:50
  25.1 16.4 %all-gather.2.cloned.1.call-done = bf16[8192,128]{1,0:T(8,128)(2,1)} async-done(((bf16[1024,128]{1,0:T(8,128)(2,1)}), bf16[8192,128]{1,0:T(8,128)(2,1)}) %all-gather.2.cloned.1.call-update) | async-done | bytes 2097168 | tf_op jit(solution)/shard_map/all_gather | solution.py:62
  41.5 14.6 %multiply_reduce_fusion = (f32[1024]{0:T(1024)S(1)}, f32[1024,8192]{1,0:T(8,128)}) fusion(bf16[1024,128]{1,0:T(8,128)(2,1)S(1)} %bitcast.39, bf16[8192,128]{1,0:T(8,128)(2,1)} %all-gather.2.cloned.1.call-done), kind=kOutput, calls=%fused_computation.5 | convolution fusion | flops 2164259840 | bytes 35917824 | tf_op jit(solution)/shard_map/dot_general | solution.py:56
  56.1 0.0 copy-start
  56.1 15.0 %convert_reduce_fusion = (f32[1024]{0:T(1024)S(1)}, bf16[1024,8192]{1,0:T(8,128)(2,1)S(1)}) fusion(f32[1024]{0:T(1024)S(1)} %get-tuple-element.9, f32[1024,8192]{1,0:T(8,128)} %get-tuple-element.10), kind=kLoop, calls=%fused_computation.3 | loop fusion | flops 41942016 | bytes 50339840 | tf_op jit(solution)/shard_map/reduce_sum | solution.py:64
  71.1 0.0 copy-done
  71.1 4.5 %subtract_convert_fusion = (bf16[1024,128]{1,0:T(8,128)(2,1)S(1)}, bf16[1024,128]{1,0:T(8,128)(2,1)S(1)}) fusion(bf16[4,256,128]{2,1,0:T(8,128)(2,1)S(1)} %all-to-all-done, f32[1024]{0:T(1024)S(1)} %get-tuple-element.2, bf16[1024,8192]{1,0:T(8,128)(2,1)S(1)} %get-tuple-element.3, bf16[8192,128]{1,0:T(8,128)(2,1)S(1)} %copy-done), kind=kOutput, calls=%fused_computation.16 | convolution fusion | flops 2148270080 | bytes 19664896 | tf_op jit(solution)/shard_map/dot_general | solution.py:65
  75.6 1.5 %collective-permute-start = (bf16[1,2,1,256,128]{4,3,0,2,1:T(8,128)(2,1)S(1)}, bf16[1,2,1,256,128]{4,3,0,2,1:T(8,128)(2,1)S(1)}, u32[]{:S(2)}, u32[]{:S(2)}) collective-permute-start(bf16[1,2,1,256,128]{4,3,0,2,1:T(8,128)(2,1)S(1)} %get-tuple-element.7), channel_id=1, source_target_pairs={{0,8},{8,16},{16,24},{24,0},{1,9},{9,17},{17,25},{25,1},{2,10},{10... | collective-permute-start | bytes 393224 | tf_op jit(solution)/shard_map/ppermute | solution.py:32
  77.2 1.5 %collective-permute-start.1 = (bf16[1,2,1,256,128]{4,3,0,2,1:T(8,128)(2,1)S(1)}, bf16[1,2,1,256,128]{4,3,0,2,1:T(8,128)(2,1)S(1)}, u32[]{:S(2)}, u32[]{:S(2)}) collective-permute-start(bf16[1,2,1,256,128]{4,3,0,2,1:T(8,128)(2,1)S(1)} %get-tuple-element.8), channel_id=1, source_target_pairs={{0,16},{8,24},{16,0},{24,8},{1,17},{9,25},{17,1},{25,9},{2,18},{10... | collective-permute-start | bytes 393224 | tf_op jit(solution)/shard_map/ppermute | solution.py:32
  78.6 0.1 fusion.1
  78.7 1.5 %collective-permute-start.2 = (bf16[1,2,1,256,128]{4,3,0,2,1:T(8,128)(2,1)S(1)}, bf16[1,2,1,256,128]{4,3,0,2,1:T(8,128)(2,1)S(1)}, u32[]{:S(2)}, u32[]{:S(2)}) collective-permute-start(bf16[1,2,1,256,128]{4,3,0,2,1:T(8,128)(2,1)S(1)} %get-tuple-element.6), channel_id=1, source_target_pairs={{0,24},{8,0},{16,8},{24,16},{1,25},{9,1},{17,9},{25,17},{2,26},{10... | collective-permute-start | bytes 393224 | tf_op jit(solution)/shard_map/ppermute | solution.py:32
  80.2 2.8 %collective-permute-done = bf16[1,2,1,256,128]{4,3,0,2,1:T(8,128)(2,1)S(1)} collective-permute-done((bf16[1,2,1,256,128]{4,3,0,2,1:T(8,128)(2,1)S(1)}, bf16[1,2,1,256,128]{4,3,0,2,1:T(8,128)(2,1)S(1)}, u32[]{:S(2)}, u32[]{:S(2)}) %collective-permute-start) | collective-permute-done | bytes 131104 | tf_op jit(solution)/shard_map/ppermute | solution.py:32
  83.0 2.0 %collective-permute-done.1 = bf16[1,2,1,256,128]{4,3,0,2,1:T(8,128)(2,1)S(1)} collective-permute-done((bf16[1,2,1,256,128]{4,3,0,2,1:T(8,128)(2,1)S(1)}, bf16[1,2,1,256,128]{4,3,0,2,1:T(8,128)(2,1)S(1)}, u32[]{:S(2)}, u32[]{:S(2)}) %collective-permute-start.1) | collective-permute-done | bytes 131104 | tf_op jit(solution)/shard_map/ppermute | solution.py:32
  85.1 0.0 collective-permute-done.2
  85.1 1.9 %gather_fusion = bf16[512,128]{1,0:T(8,128)(2,1)} fusion(bf16[1024,128]{1,0:T(8,128)(2,1)S(1)} %bitcast.37, s32[1024]{0:T(1024)S(1)} %pad_clamp_fusion), kind=kCustom, calls=%fused_computation | custom fusion | bytes 264192 | tf_op jit(solution)/shard_map/gather | solution.py:71
  87.1 1.9 %gather_fusion.1 = bf16[512,128]{1,0:T(8,128)(2,1)} fusion(bf16[1024,128]{1,0:T(8,128)(2,1)S(1)} %bitcast.36, s32[1024]{0:T(1024)S(1)} %pad_clamp_fusion), kind=kCustom, calls=%fused_computation.1 | custom fusion | bytes 264192 | tf_op jit(solution)/shard_map/gather | solution.py:71
  (6 shorter events, 0.1 us)
Async XLA Ops:
  7.2 34.3 %all-gather.2.cloned.1.call-start = ((), (), s32[]{:S(2)}) async-start(), calls=%async_computation.1 | async-start | bytes 2359296 | tf_op jit(solution)/shard_map/all_gather | solution.py:62
  14.5 10.6 %all-to-all-start = ((bf16[4,256,128]{2,1,0:T(8,128)(2,1)}), bf16[4,256,128]{2,1,0:T(8,128)(2,1)S(1)}, u32[]{:S(2)}, u32[]{:S(2)}) async-start(bf16[4,256,128]{2,1,0:T(8,128)(2,1)} %bitcast.2), calls=%async_computation | async-start | bytes 524288 | tf_op jit(solution)/shard_map/all_to_all | solution.py:50
  56.1 15.0 %copy-start = (bf16[8192,128]{1,0:T(8,128)(2,1)S(1)}, bf16[8192,128]{1,0:T(8,128)(2,1)}, u32[]{:S(2)}) copy-start(bf16[8192,128]{1,0:T(8,128)(2,1)} %all-gather.2.cloned.1.call-done) | copy-start | bytes 6291460
  75.6 7.4 %collective-permute-start = (bf16[1,2,1,256,128]{4,3,0,2,1:T(8,128)(2,1)S(1)}, bf16[1,2,1,256,128]{4,3,0,2,1:T(8,128)(2,1)S(1)}, u32[]{:S(2)}, u32[]{:S(2)}) collective-permute-start(bf16[1,2,1,256,128]{4,3,0,2,1:T(8,128)(2,1)S(1)} %get-tuple-element.7), channel_id=1, source_target_pairs={{0,8},{8,16},{16,24},{24,0},{1,9},{9,17},{17,25},{25,1},{2,10},{10... | collective-permute-start | bytes 393224 | tf_op jit(solution)/shard_map/ppermute | solution.py:32
  77.2 7.9 %collective-permute-start.1 = (bf16[1,2,1,256,128]{4,3,0,2,1:T(8,128)(2,1)S(1)}, bf16[1,2,1,256,128]{4,3,0,2,1:T(8,128)(2,1)S(1)}, u32[]{:S(2)}, u32[]{:S(2)}) collective-permute-start(bf16[1,2,1,256,128]{4,3,0,2,1:T(8,128)(2,1)S(1)} %get-tuple-element.8), channel_id=1, source_target_pairs={{0,16},{8,24},{16,0},{24,8},{1,17},{9,25},{17,1},{25,9},{2,18},{10... | collective-permute-start | bytes 393224 | tf_op jit(solution)/shard_map/ppermute | solution.py:32
  78.7 6.4 %collective-permute-start.2 = (bf16[1,2,1,256,128]{4,3,0,2,1:T(8,128)(2,1)S(1)}, bf16[1,2,1,256,128]{4,3,0,2,1:T(8,128)(2,1)S(1)}, u32[]{:S(2)}, u32[]{:S(2)}) collective-permute-start(bf16[1,2,1,256,128]{4,3,0,2,1:T(8,128)(2,1)S(1)} %get-tuple-element.6), channel_id=1, source_target_pairs={{0,24},{8,0},{16,8},{24,16},{1,25},{9,1},{17,9},{25,17},{2,26},{10... | collective-permute-start | bytes 393224 | tf_op jit(solution)/shard_map/ppermute | solution.py:32
Sparse Core Ops, SparseCore 0:
  9.6 31.8 all-gather.1
